TPU v7x, 512 devices: a whole 4x8x8 slice. The times are simulated.
512 devices in a mesh: seq: 64 (over z, x, core), head: 8 (over y).
Axes of the slice: x: 4, y: 8, z: 8, core: 2. Of those that a mesh axis runs over, the one named last changes fastest.
Arguments:
- projected: float32 [65536, 2560], P(('seq', 'head')), may hold values from -6 to 6
- out_grads: float32 [65536, 2048], P(('seq', 'head')), may hold values from -6 to 6
- conv_weight: float32 [3, 2560], replicated, may hold values from -2.4 to 2.4
- doc_lengths: int32 [16], replicated, may hold values from 1 to 32768, 65536 in all
Outputs:
- grad_projected: float32 [65536, 2560], P(('seq', 'head'))
- grad_conv: float32 [3, 2560], replicated
Inputs may be any that keep to these rules, and one draw needn't show every extreme that they name: `doc_lengths`: the 16 documents fill the 65536 tokens end to end; the longest holds exactly half of 65536 tokens.
All inputs are finite; a program needn't handle non-finite values.
Results may differ from a plain program's by a relative error of at most 0.0003.
Values sent between devices are 32-bit elements; how exact they have to be, the bound alone decides.
No kernel may reach another device: no remote copies, remote signals or barrier semaphores. Data moves between devices by JAX's collectives and lax.ppermute only.
A program may use at most 128 MiB of HBM per device.

v0:
```python
import math
import jax
import jax.numpy as jnp
import numpy as np
from jax import lax
from jax.sharding import PartitionSpec as P

KEY_DIM = 16
HEAD_DIM = 128
HIGHEST = lax.Precision.HIGHEST


def carried_in(x, axis, combine, identity, reverse):
    length, here = (lax.axis_size(axis), lax.axis_index(axis))
    everything = jax.tree.map(lambda part: lax.all_gather(part, axis), x)
    start = jax.tree.map(
        lambda part, zero: jnp.broadcast_to(jnp.asarray(zero, part.dtype), part.shape), x, identity
    )

    def lap(k, before):
        at = length - 1 - k if reverse else k
        reached = at > here if reverse else at < here
        new = combine(before, jax.tree.map(lambda part: part[at], everything))
        return jax.tree.map(lambda a, b: jnp.where(reached, a, b), new, before)

    return lax.fori_loop(0, length, lap, start)


def passed_along(value, axis, steps):
    count = lax.axis_size(axis)
    initial, last = (max(0, -steps), min(count, count - steps))
    return lax.ppermute(value, axis, [(source, source + steps) for source in range(initial, last)])


def feature_map(columns):
    key_size = columns.shape[1]
    upper_i, upper_j = np.triu_indices(key_size)
    factors = np.where(upper_i == upper_j, 1.0 / math.sqrt(2.0), 1.0).astype(np.float32)
    products = columns[:, upper_i, :] * columns[:, upper_j, :] * jnp.asarray(factors)[None, :, None]
    constant = jnp.ones((columns.shape[0], 1, columns.shape[2]), jnp.float32)
    return jnp.concatenate([constant, columns, products], axis=1)


def doc_place(doc_lengths, anchor, amount):
    positions = anchor + jnp.arange(amount, dtype=jnp.int32)
    starts = jnp.cumsum(doc_lengths) - doc_lengths
    begins = jnp.max(jnp.where(starts[None, :] <= positions[:, None], starts[None, :], 0), axis=1)
    return (begins, positions - begins)


def conv_forward(signal, leading, weights, offsets):
    row_count = signal.shape[0]
    behind = jnp.concatenate([leading, signal], axis=0)
    back_one = behind[1 : row_count + 1] * (offsets[0:row_count] >= 1).astype(jnp.float32)[:, None]
    back_two = behind[0:row_count] * (offsets[0:row_count] >= 2).astype(jnp.float32)[:, None]
    return weights[0] * signal + weights[1] * back_one + weights[2] * back_two


def conv_backward(grad_rows, trailing, signal, leading, weights, offsets):
    row_count = grad_rows.shape[0]
    ahead_rows = jnp.concatenate([grad_rows, trailing], axis=0)
    ahead_one = (
        ahead_rows[1 : row_count + 1]
        * (offsets[1 : row_count + 1] >= 1).astype(jnp.float32)[:, None]
    )
    ahead_two = (
        ahead_rows[2 : row_count + 2]
        * (offsets[2 : row_count + 2] >= 2).astype(jnp.float32)[:, None]
    )
    grad_signal = weights[0] * grad_rows + weights[1] * ahead_one + weights[2] * ahead_two
    behind = jnp.concatenate([leading, signal], axis=0)
    own_one = (offsets[0:row_count] >= 1).astype(jnp.float32)[:, None]
    own_two = (offsets[0:row_count] >= 2).astype(jnp.float32)[:, None]
    grad_weights = jnp.stack(
        [
            jnp.sum(grad_rows * signal, axis=0),
            jnp.sum(grad_rows * behind[1 : row_count + 1] * own_one, axis=0),
            jnp.sum(grad_rows * behind[0:row_count] * own_two, axis=0),
        ],
        axis=0,
    )
    return (grad_signal, grad_weights)


def combine(earlier, following):
    carry_keep = 1.0 - following[2]
    return (
        following[0] + carry_keep[:, None, None] * earlier[0],
        following[1] + carry_keep[:, None] * earlier[1],
        jnp.maximum(earlier[2], following[2]),
    )


def attention_grads(mixed_rows, out_flat, begins, stretch_start):
    length = mixed_rows.shape[0]
    head_width = 2 * KEY_DIM + HEAD_DIM
    local_heads = mixed_rows.shape[1] // head_width
    block_len = min(128, length)
    blocks = length // block_len
    scale_key = KEY_DIM ** (-0.25)
    shaped = mixed_rows.reshape(length, local_heads, head_width)
    query_cols = jnp.transpose(shaped[:, :, :KEY_DIM], (1, 2, 0)) * scale_key
    key_cols = jnp.transpose(shaped[:, :, KEY_DIM : 2 * KEY_DIM], (1, 2, 0)) * scale_key
    values = shaped[:, :, 2 * KEY_DIM :]
    upstream = out_flat.reshape(length, local_heads, HEAD_DIM)
    query_feat, query_pull = jax.vjp(feature_map, query_cols)
    key_feat, key_pull = jax.vjp(feature_map, key_cols)
    feat_count = query_feat.shape[1]
    last_begin = begins[length - 1]
    has_start = (last_begin >= stretch_start).astype(jnp.float32).reshape(1)
    tail_mask = (begins == last_begin).astype(jnp.float32)
    tail_feat = key_feat * tail_mask[None, None, :]
    tail_state = jnp.einsum("hfl,lhe->hfe", tail_feat, values, precision=HIGHEST)
    tail_norm = jnp.sum(tail_feat, axis=2)
    identity = (jnp.zeros_like(tail_state), jnp.zeros_like(tail_norm), jnp.zeros((1,), jnp.float32))
    prefix = carried_in((tail_state, tail_norm, has_start), "seq", combine, identity, False)
    causal = jnp.arange(block_len)[:, None] >= jnp.arange(block_len)[None, :]
    indices = jnp.arange(blocks, dtype=jnp.int32)

    def forward_block(carried, block_index):
        carry_state, carry_norm = carried
        offset_rows = block_index * block_len
        block_start = stretch_start + offset_rows
        query_blk = lax.dynamic_slice_in_dim(query_feat, offset_rows, block_len, 2)
        key_blk = lax.dynamic_slice_in_dim(key_feat, offset_rows, block_len, 2)
        value_blk = lax.dynamic_slice_in_dim(values, offset_rows, block_len, 0)
        doc_blk = lax.dynamic_slice_in_dim(begins, offset_rows, block_len, 0)
        allowed = causal & (doc_blk[:, None] == doc_blk[None, :])
        scores = jnp.where(
            allowed[None], jnp.einsum("hft,hfs->hts", query_blk, key_blk, precision=HIGHEST), 0.0
        )
        from_carry = (doc_blk < block_start).astype(jnp.float32)
        numerator = jnp.einsum("hts,she->the", scores, value_blk, precision=HIGHEST) + from_carry[
            :, None, None
        ] * jnp.einsum("hft,hfe->the", query_blk, carry_state, precision=HIGHEST)
        denominator = jnp.sum(scores, axis=2) + from_carry[None, :] * jnp.einsum(
            "hft,hf->ht", query_blk, carry_norm, precision=HIGHEST
        )
        block_tail = (doc_blk == doc_blk[block_len - 1]).astype(jnp.float32)
        carry_keep = (doc_blk[block_len - 1] < block_start).astype(jnp.float32)
        tail_keys = key_blk * block_tail[None, None, :]
        next_state = (
            jnp.einsum("hfs,she->hfe", tail_keys, value_blk, precision=HIGHEST)
            + carry_keep * carry_state
        )
        next_norm = jnp.sum(tail_keys, axis=2) + carry_keep * carry_norm
        return ((next_state, next_norm), (numerator, denominator, carry_state, carry_norm, scores))

    forward_out = lax.scan(forward_block, (prefix[0], prefix[1]), indices)
    numerators, denominators, states, norms, kept_scores = forward_out[1]
    denom_rows = jnp.transpose(denominators, (0, 2, 1)).reshape(length, local_heads)
    attended = numerators.reshape(length, local_heads, HEAD_DIM) / denom_rows[:, :, None]
    grad_num = upstream / denom_rows[:, :, None]
    scalar_grad = -jnp.sum(upstream * attended, axis=2) / denom_rows
    lead_mask = (begins < stretch_start).astype(jnp.float32)
    lead_feat = query_feat * lead_mask[None, None, :]
    lead_state = jnp.einsum("hfl,lhe->hfe", lead_feat, grad_num, precision=HIGHEST)
    lead_norm = jnp.einsum("hfl,lh->hf", lead_feat, scalar_grad, precision=HIGHEST)
    suffix = carried_in((lead_state, lead_norm, has_start), "seq", combine, identity, True)

    def backward_block(carried, inputs):
        back_state, back_norm = carried
        block_index, carry_state, carry_norm, scores = inputs
        offset_rows = block_index * block_len
        block_start = stretch_start + offset_rows
        query_blk = lax.dynamic_slice_in_dim(query_feat, offset_rows, block_len, 2)
        key_blk = lax.dynamic_slice_in_dim(key_feat, offset_rows, block_len, 2)
        value_blk = lax.dynamic_slice_in_dim(values, offset_rows, block_len, 0)
        doc_blk = lax.dynamic_slice_in_dim(begins, offset_rows, block_len, 0)
        grad_blk = lax.dynamic_slice_in_dim(grad_num, offset_rows, block_len, 0)
        scalar_blk = lax.dynamic_slice_in_dim(scalar_grad, offset_rows, block_len, 0)
        scalar_cols = scalar_blk.T
        allowed = causal & (doc_blk[:, None] == doc_blk[None, :])
        dscores = jnp.where(
            allowed[None],
            jnp.einsum("the,she->hts", grad_blk, value_blk, precision=HIGHEST)
            + scalar_cols[:, :, None],
            0.0,
        )
        from_carry = (doc_blk < block_start).astype(jnp.float32)
        block_tail = (doc_blk == doc_blk[block_len - 1]).astype(jnp.float32)
        carry_keep = (doc_blk[block_len - 1] < block_start).astype(jnp.float32)
        grad_query = jnp.einsum("hts,hfs->hft", dscores, key_blk, precision=HIGHEST) + from_carry[
            None, None, :
        ] * (
            jnp.einsum("hfe,the->hft", carry_state, grad_blk, precision=HIGHEST)
            + carry_norm[:, :, None] * scalar_cols[:, None, :]
        )
        grad_key = jnp.einsum("hts,hft->hfs", dscores, query_blk, precision=HIGHEST) + block_tail[
            None, None, :
        ] * (
            jnp.einsum("hfe,she->hfs", back_state, value_blk, precision=HIGHEST)
            + back_norm[:, :, None]
        )
        grad_value = jnp.einsum("hts,the->she", scores, grad_blk, precision=HIGHEST) + block_tail[
            :, None, None
        ] * jnp.einsum("hfs,hfe->she", key_blk, back_state, precision=HIGHEST)
        lead_blk = query_blk * from_carry[None, None, :]
        next_state = (
            jnp.einsum("hft,the->hfe", lead_blk, grad_blk, precision=HIGHEST)
            + carry_keep * back_state
        )
        next_norm = (
            jnp.einsum("hft,th->hf", lead_blk, scalar_blk, precision=HIGHEST)
            + carry_keep * back_norm
        )
        return ((next_state, next_norm), (grad_query, grad_key, grad_value))

    swept_back = lax.scan(
        backward_block, (suffix[0], suffix[1]), (indices, states, norms, kept_scores), reverse=True
    )
    grad_qblocks, grad_kblocks, grad_vblocks = swept_back[1]
    query_grad = jnp.transpose(grad_qblocks, (1, 2, 0, 3)).reshape(local_heads, feat_count, length)
    key_grad = jnp.transpose(grad_kblocks, (1, 2, 0, 3)).reshape(local_heads, feat_count, length)
    value_grad = grad_vblocks.reshape(length, local_heads, HEAD_DIM)
    query_in = jnp.transpose(query_pull(query_grad)[0] * scale_key, (2, 0, 1))
    key_in = jnp.transpose(key_pull(key_grad)[0] * scale_key, (2, 0, 1))
    return jnp.concatenate([query_in, key_in, value_grad], axis=2).reshape(
        length, local_heads * head_width
    )


def on_device(projected, out_grads, conv_weight, doc_lengths):
    row_count = projected.shape[0]
    head_count = lax.axis_size("head")
    seq_index = lax.axis_index("seq")
    head_index = lax.axis_index("head")
    group_len = row_count * head_count
    token_base = (seq_index * head_count + head_index) * row_count
    stretch_start = seq_index * group_len
    token_begins, token_offsets = doc_place(doc_lengths, token_base, row_count + 2)
    leading = passed_along(projected[row_count - 2 :], ("seq", "head"), 1)
    outgoing = conv_forward(projected, leading, conv_weight, token_offsets)
    arrived, upstream = (
        lax.all_to_all(outgoing, "head", split_axis=1, concat_axis=0, tiled=True),
        lax.all_to_all(out_grads, "head", split_axis=1, concat_axis=0, tiled=True),
    )
    group_begins, group_offsets = doc_place(doc_lengths, stretch_start, group_len + 2)
    grad_mixed = attention_grads(arrived, upstream, group_begins[:group_len], stretch_start)
    returned = lax.all_to_all(grad_mixed, "head", split_axis=0, concat_axis=1, tiled=True)
    trailing = passed_along(returned[:2], ("seq", "head"), -1)
    grad_projected, weight_part = conv_backward(
        returned, trailing, projected, leading, conv_weight, token_offsets
    )
    grad_conv = lax.psum(weight_part, ("seq", "head"))
    return (grad_projected, grad_conv)


def solution(mesh):
    return jax.shard_map(
        on_device,
        mesh=mesh,
        in_specs=(P(("seq", "head"), None), P(("seq", "head"), None), P(), P()),
        out_specs=(P(("seq", "head"), None), P()),
        check_vma=False,
    )
```

profile of v0, /device:TPU:1, one launch (start us, length us, event | category | flops | bytes accessed | tf_op | source)
XLA Modules:
  0.0 1203.6 jit_solution(1783652886522364890)
XLA Ops:
  8.1 4.0 collective-permute-start
  17.7 3.1 multiply_add_fusion.1
  20.8 6.1 all-to-all-start
  28.4 33.2 %all-to-all-done = f32[128,8,320]{0,2,1:T(8,128)S(1)} async-done(((f32[128,8,320]{0,2,1:T(8,128)}), f32[128,8,320]{0,2,1:T(8,128)S(1)}, u32[]{:S(2)}, u32[]{:S(2)}) %all-to-all-start) | async-done | bytes 1310752 | tf_op jit(solution)/shard_map/all_to_all | solution.py:235
  64.6 3.1 gather_fusion.1
  73.7 3.1 fusion.91
  76.8 4.8 broadcast_multiply_fusion.1
  85.3 3.6 all-to-all-start.1
  91.7 131.3 %all-reduce = f32[64]{0:T(128)S(1)} all-reduce(f32[64]{0:T(128)S(1)} %dynamic-update-slice), channel_id=1, replica_groups=mesh['seq'=64,'head'=8] {'seq'}, use_global_device_ids=true, to_apply=%add | all-reduce | flops 64 | bytes 512
  232.5 51.4 %all-gather.4 = f32[64,2,153]{2,1,0:T(2,128)S(1)} all-gather(f32[1,2,153]{2,1,0:T(2,128)S(1)} %copy.127), channel_id=3, replica_groups=mesh['seq'=64,'head'=8] {'seq'}, dimensions={0}, use_global_device_ids=true | all-gather | bytes 79560 | tf_op jit(solution)/shard_map/all_gather | solution.py:15
  283.9 187.7 %while.82 = (s32[]{:T(128)}, f32[2,153,128]{2,1,0:T(8,128)S(1)}, f32[2,153]{1,0:T(2,128)S(1)}, s32[]{:T(128)}, f32[64,2,153,128]{3,2,1,0:T(8,128)}, /*index=5*/f...) while((s32[]{:T(128)}, f32[2,153,128]{2,1,0:T(8,128)S(1)}, ...), condition=%wide.region_5.6_spmd.clone, body=%wide.region_4.5_spmd.clone.sunk | while | flops 157901 | bytes 473831 | solution.py:26
  472.9 110.3 %while.80 = (s32[]{:T(128)}, f32[2,153,128]{2,1,0:T(8,128)S(1)}, f32[2,153]{1,0:T(2,128)S(1)}, f32[8,128,2,128]{1,0,3,2:T(8,128)}, f32[8,2,128]{2,1,0:T(2,128)S(...) while((s32[]{:T(128)}, f32[2,153,128]{2,1,0:T(8,128)S(1)}, ...), condition=%wide.region_9.10_spmd.clone, body=%wide.region_6.9_spmd.clone.sunk | while | flops 231664960 | bytes 3280461 | solution.py:149
  476.9 4.8 dynamic_update_slice.74
  490.7 4.8 dynamic_update_slice.74
  504.5 4.8 dynamic_update_slice.74
  518.3 4.8 dynamic_update_slice.74
  532.1 4.8 dynamic_update_slice.74
  545.9 4.8 dynamic_update_slice.74
  559.7 4.8 dynamic_update_slice.74
  573.4 4.8 dynamic_update_slice.74
  593.5 49.5 %all-gather.5 = f32[64,2,153]{2,1,0:T(2,128)S(1)} all-gather(f32[1,2,153]{2,1,0:T(2,128)S(1)} %bitcast.282), channel_id=5, replica_groups=mesh['seq'=64,'head'=8] {'seq'}, dimensions={0}, use_global_device_ids=true | all-gather | bytes 79560 | tf_op jit(solution)/shard_map/all_gather | solution.py:15
  643.0 36.5 %all-gather.11.cloned.1.call-done = f32[128,153,128]{2,1,0:T(8,128)} async-done(((f32[2,153,128]{2,1,0:T(8,128)}), f32[128,153,128]{2,1,0:T(8,128)}) %all-gather.11.cloned.1.call-update) | async-done | bytes 10027024 | tf_op jit(solution)/shard_map/all_gather | solution.py:15
  679.5 195.2 %while.83 = (s32[]{:T(128)}, f32[2,153,128]{2,1,0:T(8,128)S(1)}, f32[2,153]{1,0:T(2,128)S(1)}, s32[]{:T(128)}, f32[64,2,153,128]{3,2,1,0:T(8,128)}, /*index=5*/f...) while((s32[]{:T(128)}, f32[2,153,128]{2,1,0:T(8,128)S(1)}, ...), condition=%wide.region_12.13_spmd.clone, body=%wide.region_11.12_spmd.clone.sunk | while | flops 157905 | bytes 473893 | solution.py:26
  878.2 112.1 %while.81 = (s32[]{:T(128)}, f32[2,153,128]{2,1,0:T(8,128)S(1)}, f32[2,153]{1,0:T(2,128)S(1)}, f32[8,2,153,128]{3,2,1,0:T(8,128)}, f32[8,2,153,128]{3,2,1,0:T(8,...) while((s32[]{:T(128)}, f32[2,153,128]{2,1,0:T(8,128)S(1)}, ...), condition=%wide.region_14.15_spmd.clone, body=%wide.region_13.14_spmd.clone.sunk | while | flops 462717824 | bytes 4866477 | solution.py:209
  998.9 5.9 fusion.90
  1004.9 14.0 %scatter_fusion = f32[2,16,1024]{2,0,1:T(2,128)S(1)} fusion(f32[2,16,1024]{2,0,1:T(2,128)S(1)} %split.16, s32[136]{0:T(256)S(1)} %copy-done.23, f32[136,2,1024]{2,1,0:T(2,128)} %get-tuple-element.1103), kind=kCustom, calls=%fused_computation.4 | custom fusion | flops 278528 | bytes 3342880 | tf_op jit(solution)/shard_map/transpose(jvp())/scatter-add | solution.py:39
  1018.9 7.6 scatter_fusion.1
  1027.7 7.6 scatter_fusion.3
  1035.3 7.6 scatter_fusion.2
  1048.3 40.7 %all_to_all.51 = f32[8,128,320]{1,2,0:T(8,128)S(1)} all-to-all(f32[8,128,320]{1,2,0:T(8,128)S(1)} %copy.143), channel_id=1, replica_groups=mesh['seq'=64,'head'=8] {'head'}, dimensions={0} | all-to-all | bytes 2621440 | tf_op jit(solution)/shard_map/all_to_all | solution.py:240
  1093.7 95.5 %psum.7 = f32[3,2560]{1,0:T(4,128)} all-reduce(f32[3,2560]{1,0:T(4,128)S(1)} %pad_maximum_fusion.5), channel_id=1, replica_groups=mesh['seq'=64,'head'=8] {'seq','head'}, use_global_device_ids=true, to_apply=%region_22.23 | all-reduce | flops 7680 | bytes 61440 | tf_op jit(solution)/shard_map/psum | solution.py:245
  1190.7 4.4 fusion.77
  (830 shorter events, 611.8 us)
Async XLA Ops:
  8.1 9.1 collective-permute-start
  14.4 3.2 copy-start.25
  14.4 3.2 copy-start.27
  15.4 2.2 copy-start.16
  17.2 3.6 copy-start.3
  17.6 3.1 copy-start.5
  20.8 6.9 copy-start.24
  20.8 6.9 copy-start.23
  20.8 40.9 %all-to-all-start = ((f32[128,8,320]{0,2,1:T(8,128)}), f32[128,8,320]{0,2,1:T(8,128)S(1)}, u32[]{:S(2)}, u32[]{:S(2)}) async-start(f32[128,8,320]{0,2,1:T(8,128)} %bitcast.265), calls=%async_computation | async-start | bytes 2621440 | tf_op jit(solution)/shard_map/all_to_all | solution.py:235
  26.9 257.1 %all-gather.9.cloned.1.call-start = ((), (), s32[]{:S(2)}) async-start(), calls=%async_computation.3 | async-start | bytes 10649600 | tf_op jit(solution)/shard_map/all_gather | solution.py:15
  27.0 62.6 %copy-start.22 = (s32[1026]{0:T(1024)}, s32[1026]{0:T(1024)S(1)}, u32[]{:S(2)}) copy-start(s32[1026]{0:T(1024)S(1)} %select_reduce_fusion) | copy-start | bytes 12316
  64.6 9.1 copy-start.7
  70.7 3.0 copy-start.29
  81.6 2.3 copy-start.15
  85.3 137.7 %all-to-all-start.1 = ((f32[128,8,256]{0,2,1:T(8,128)}), f32[128,8,256]{0,2,1:T(8,128)S(1)}, u32[]{:S(2)}, u32[]{:S(2)}) async-start(f32[128,8,256]{0,2,1:T(8,128)} %bitcast.273), calls=%async_computation.1 | async-start | bytes 2097152 | tf_op jit(solution)/shard_map/all_to_all | solution.py:236
  88.8 590.7 %all-gather.11.cloned.1.call-start = ((), (), s32[]{:S(2)}) async-start(), calls=%async_computation.4 | async-start | bytes 10649600 | tf_op jit(solution)/shard_map/all_gather | solution.py:15
  585.5 2.9 copy-start.2
  995.9 3.1 copy-start.8
  997.8 7.0 copy-start.1
  1004.9 14.0 %copy-start.14 = (f32[136,2,1024]{2,1,0:T(2,128)S(1)}, f32[136,2,1024]{2,1,0:T(2,128)}, u32[]{:S(2)}) copy-start(f32[136,2,1024]{2,1,0:T(2,128)} %get-tuple-element.1102) | copy-start | bytes 3342340
  1027.7 7.6 slice-start
  1027.7 7.6 copy-start.12
  1048.0 41.0 %copy-start.26 = (f32[128]{0:T(128)S(1)}, f32[128]{0:T(128)}, u32[]{:S(2)}) copy-start(f32[128]{0:T(128)} %copy-done.25) | copy-start | bytes 1540
  1048.1 41.0 %copy-start.28 = (f32[128]{0:T(128)S(1)}, f32[128]{0:T(128)}, u32[]{:S(2)}) copy-start(f32[128]{0:T(128)} %copy-done.27) | copy-start | bytes 1540
  1048.3 40.7 %copy-start.4 = (f32[128,2560]{0,1:T(8,128)S(1)}, f32[128,2560]{0,1:T(8,128)}, u32[]{:S(2)}) copy-start(f32[128,2560]{0,1:T(8,128)} %copy-done.3) | copy-start | bytes 3932164
  1048.3 40.7 %copy-start.6 = (f32[2,2560]{0,1:T(8,128)S(1)}, f32[2,2560]{0,1:T(8,128)}, u32[]{:S(2)}) copy-start(f32[2,2560]{0,1:T(8,128)} %copy-done.5) | copy-start | bytes 61444
  1091.3 99.4 %copy-start.17 = (f32[2560]{0:T(1024)S(1)}, f32[2560]{0:T(1024)}, u32[]{:S(2)}) copy-start(f32[2560]{0:T(1024)} %copy-done.16) | copy-start | bytes 30724
  1091.3 99.4 %copy-start.19 = (f32[2560]{0:T(1024)S(1)}, f32[2560]{0:T(1024)}, u32[]{:S(2)}) copy-start(f32[2560]{0:T(1024)} %copy-done.18) | copy-start | bytes 30724
  1091.3 99.4 %copy-start.21 = (f32[2560]{0:T(1024)S(1)}, f32[2560]{0:T(1024)}, u32[]{:S(2)}) copy-start(f32[2560]{0:T(1024)} %copy-done.20) | copy-start | bytes 30724
  1091.3 99.4 %copy-start.30 = (f32[128]{0:T(128)S(1)}, f32[128]{0:T(128)}, u32[]{:S(2)}) copy-start(f32[128]{0:T(128)} %get-tuple-element.1110) | copy-start | bytes 1540
  1091.3 99.4 %copy-start.31 = (f32[128]{0:T(128)S(1)}, f32[128]{0:T(128)}, u32[]{:S(2)}) copy-start(f32[128]{0:T(128)} %get-tuple-element.1112) | copy-start | bytes 1540
  1091.7 97.5 %collective-permute-start.1 = (f32[2,2560]{1,0:T(2,128)S(1)}, f32[2,2560]{1,0:T(2,128)S(1)}, u32[]{:S(2)}, u32[]{:S(2)}) collective-permute-start(f32[2,2560]{1,0:T(2,128)S(1)} %copy.144), channel_id=1, source_target_pairs={{1,0},{2,1},{3,2},{4,3},{5,4},{6,5},{7,6},{8,7},{9,8},{10,9},{11,1... | collective-permute-start | bytes 61448 | tf_op jit(solution)/shard_map/ppermute | solution.py:32
  (8 other events, 12.7 us)
Sparse Core Ops, SparseCore 0:
  84.0 91.8 all-gather.8
  590.8 88.6 all-gather.10
where the time goes:
time: 1220 us; the launch traced here: 1200 us
  other arithmetic  462 us (38%)
  blocking collectives  368 us (30%)
  local copies, waits for them, and re-layouts  129 us (11%)
  matrix products  118 us (10%)
  waiting for transfers between devices  69.8 us (6%)
  loops' own time  25.3 us (2%)
  starting transfers between devices  15.7 us (1%)
  between operations  15.7 us (1%)
    select_n x256, other arithmetic, lap(): return jax.tree.map(lambda a, b: jnp.where(reached, a, b), new, before)  301 us
    unnamed x1, blocking collectives  131 us
    all_gather x2, blocking collectives, carried_in(): everything = jax.tree.map(lambda part: lax.all_gather(part, axis), x)  101 us
    psum x1, blocking collectives, on_device(): grad_conv = lax.psum(weight_part, ('seq', 'head'))  95.5 us
    sub x128, other arithmetic, combine(): carry_keep = 1.0 - following[2]  78.9 us
    dynamic_update_slice x48, local copies, waits for them, and re-layouts, attention_grads(): forward_out = lax.scan(forward_block, (prefix[0], prefix[1]), indices)  55 us
    all_to_all x1, blocking collectives, on_device(): lax.all_to_all(grad_mixed, 'head', split_axis=0, concat_axis=1, tiled=True)  40.7 us
    all_gather x2, waiting for transfers between devices, carried_in(): everything = jax.tree.map(lambda part: lax.all_gather(part, axis), x)  36.5 us
  transfers between devices with their start and end apart: 6, of which 2 were waited for; matrix products, arithmetic and copies ran while one was open for 2% of the time, Pallas kernels for 0%

commit v1 on v0

--- a/solution.py
+++ b/solution.py
@@ -242,7 +242,7 @@
     grad_projected, weight_part = conv_backward(
         returned, trailing, projected, leading, conv_weight, token_offsets
     )
-    grad_conv = lax.psum(weight_part, ("seq", "head"))
+    grad_conv = lax.psum(lax.psum(weight_part, "head"), "seq")
     return (grad_projected, grad_conv)
 
 

time: 1220 us -> 1390 us (1.14)
  blocking collectives: 368 us -> 544 us
    psum x1 -> x2, blocking collectives: 95.5 us -> 271 us  [on_device(): grad_conv = lax.psum(lax.psum(weight_part, 'head'), 'seq')]
  transfers between devices with their start and end apart: 6 -> 6, of which waited for: 2 -> 2; matrix products, arithmetic and copies ran while one was open for 2% -> 1% of each run, Pallas kernels for 0% -> 0%
where the time goes in v1:
time: 1390 us; the launch traced here: 1380 us
  blocking collectives  544 us (39%)
  other arithmetic  451 us (32%)
  local copies, waits for them, and re-layouts  135 us (10%)
  matrix products  118 us (8%)
  waiting for transfers between devices  69.8 us (5%)
  loops' own time  25.9 us (2%)
  starting transfers between devices  15.7 us (1%)
  between operations  15.6 us (1%)
    select_n x256, other arithmetic, lap(): return jax.tree.map(lambda a, b: jnp.where(reached, a, b), new, before)  294 us
    psum x2, blocking collectives, on_device(): grad_conv = lax.psum(lax.psum(weight_part, 'head'), 'seq')  271 us
    unnamed x1, blocking collectives  132 us
    all_gather x2, blocking collectives, carried_in(): everything = jax.tree.map(lambda part: lax.all_gather(part, axis), x)  101 us
    sub x128, other arithmetic, combine(): carry_keep = 1.0 - following[2]  75.4 us
    dynamic_update_slice x48, local copies, waits for them, and re-layouts, attention_grads(): forward_out = lax.scan(forward_block, (prefix[0], prefix[1]), indices)  54.8 us
    all_to_all x1, blocking collectives, on_device(): lax.all_to_all(grad_mixed, 'head', split_axis=0, concat_axis=1, tiled=True)  40.8 us
    all_gather x2, waiting for transfers between devices, carried_in(): everything = jax.tree.map(lambda part: lax.all_gather(part, axis), x)  36.4 us
  transfers between devices with their start and end apart: 6, of which 2 were waited for; matrix products, arithmetic and copies ran while one was open for 1% of the time, Pallas kernels for 0%

profile of v1, /device:TPU:1, one launch (start us, length us, event | category | flops | bytes accessed | tf_op | source)
XLA Modules:
  0.0 1375.4 jit_solution(9665241873513913439)
XLA Ops:
  8.1 4.0 collective-permute-start
  17.0 3.1 multiply_add_fusion.1
  20.1 6.1 all-to-all-start
  27.7 33.3 %all-to-all-done = f32[128,8,320]{0,2,1:T(8,128)S(1)} async-done(((f32[128,8,320]{0,2,1:T(8,128)}), f32[128,8,320]{0,2,1:T(8,128)S(1)}, u32[]{:S(2)}, u32[]{:S(2)}) %all-to-all-start) | async-done | bytes 1310752 | tf_op jit(solution)/shard_map/all_to_all | solution.py:235
  77.0 3.4 fusion.91
  80.5 4.3 broadcast_multiply_fusion.1
  88.4 3.6 all-to-all-start.1
  94.8 131.7 %all-reduce = f32[64]{0:T(128)S(1)} all-reduce(f32[64]{0:T(128)S(1)} %dynamic-update-slice), channel_id=1, replica_groups=mesh['seq'=64,'head'=8] {'seq'}, use_global_device_ids=true, to_apply=%add | all-reduce | flops 64 | bytes 512
  236.0 51.6 %all-gather.4 = f32[64,2,153]{2,1,0:T(2,128)S(1)} all-gather(f32[1,2,153]{2,1,0:T(2,128)S(1)} %copy.127), channel_id=3, replica_groups=mesh['seq'=64,'head'=8] {'seq'}, dimensions={0}, use_global_device_ids=true | all-gather | bytes 79560 | tf_op jit(solution)/shard_map/all_gather | solution.py:15
  287.6 187.7 %while.82 = (s32[]{:T(128)}, f32[2,153,128]{2,1,0:T(8,128)S(1)}, f32[2,153]{1,0:T(2,128)S(1)}, s32[]{:T(128)}, f32[64,2,153,128]{3,2,1,0:T(8,128)}, /*index=5*/f...) while((s32[]{:T(128)}, f32[2,153,128]{2,1,0:T(8,128)S(1)}, ...), condition=%wide.region_5.6_spmd.clone, body=%wide.region_4.5_spmd.clone.sunk | while | flops 157901 | bytes 473831 | solution.py:26
  476.6 110.1 %while.80 = (s32[]{:T(128)}, f32[2,153,128]{2,1,0:T(8,128)S(1)}, f32[2,153]{1,0:T(2,128)S(1)}, f32[8,128,2,128]{1,0,3,2:T(8,128)}, f32[8,2,128]{2,1,0:T(2,128)S(...) while((s32[]{:T(128)}, f32[2,153,128]{2,1,0:T(8,128)S(1)}, ...), condition=%wide.region_9.10_spmd.clone, body=%wide.region_6.9_spmd.clone.sunk | while | flops 231664960 | bytes 3280461 | solution.py:149
  480.6 4.7 dynamic_update_slice.74
  494.4 4.7 dynamic_update_slice.74
  508.2 4.7 dynamic_update_slice.74
  521.9 4.7 dynamic_update_slice.74
  535.7 4.7 dynamic_update_slice.74
  549.5 4.7 dynamic_update_slice.74
  563.2 4.7 dynamic_update_slice.74
  577.0 4.7 dynamic_update_slice.74
  597.0 49.5 %all-gather.5 = f32[64,2,153]{2,1,0:T(2,128)S(1)} all-gather(f32[1,2,153]{2,1,0:T(2,128)S(1)} %bitcast.282), channel_id=5, replica_groups=mesh['seq'=64,'head'=8] {'seq'}, dimensions={0}, use_global_device_ids=true | all-gather | bytes 79560 | tf_op jit(solution)/shard_map/all_gather | solution.py:15
  646.5 36.4 %all-gather.11.cloned.1.call-done = f32[128,153,128]{2,1,0:T(8,128)} async-done(((f32[2,153,128]{2,1,0:T(8,128)}), f32[128,153,128]{2,1,0:T(8,128)}) %all-gather.11.cloned.1.call-update) | async-done | bytes 10027024 | tf_op jit(solution)/shard_map/all_gather | solution.py:15
  683.0 184.7 %while.83 = (s32[]{:T(128)}, f32[2,153,128]{2,1,0:T(8,128)S(1)}, f32[2,153]{1,0:T(2,128)S(1)}, s32[]{:T(128)}, f32[64,2,153,128]{3,2,1,0:T(8,128)}, /*index=5*/f...) while((s32[]{:T(128)}, f32[2,153,128]{2,1,0:T(8,128)S(1)}, ...), condition=%wide.region_12.13_spmd.clone, body=%wide.region_11.12_spmd.clone.sunk | while | flops 157905 | bytes 473893 | solution.py:26
  871.2 113.0 %while.81 = (s32[]{:T(128)}, f32[2,153,128]{2,1,0:T(8,128)S(1)}, f32[2,153]{1,0:T(2,128)S(1)}, f32[8,2,153,128]{3,2,1,0:T(8,128)}, f32[8,2,153,128]{3,2,1,0:T(8,...) while((s32[]{:T(128)}, f32[2,153,128]{2,1,0:T(8,128)S(1)}, ...), condition=%wide.region_14.15_spmd.clone, body=%wide.region_13.14_spmd.clone.sunk | while | flops 462717824 | bytes 4866477 | solution.py:209
  992.7 5.9 fusion.90
  998.7 14.0 %scatter_fusion = f32[2,16,1024]{2,0,1:T(2,128)S(1)} fusion(f32[2,16,1024]{2,0,1:T(2,128)S(1)} %split.16, s32[136]{0:T(256)S(1)} %copy-done.16, f32[136,2,1024]{2,1,0:T(2,128)} %get-tuple-element.1103), kind=kCustom, calls=%fused_computation.4 | custom fusion | flops 278528 | bytes 3342880 | tf_op jit(solution)/shard_map/transpose(jvp())/scatter-add | solution.py:39
  1012.7 7.6 scatter_fusion.1
  1021.8 7.6 scatter_fusion.3
  1029.4 7.6 scatter_fusion.2
  1044.8 40.8 %all_to_all.51 = f32[8,128,320]{1,2,0:T(8,128)S(1)} all-to-all(f32[8,128,320]{1,2,0:T(8,128)S(1)} %copy.143), channel_id=1, replica_groups=mesh['seq'=64,'head'=8] {'head'}, dimensions={0} | all-to-all | bytes 2621440 | tf_op jit(solution)/shard_map/all_to_all | solution.py:240
  1090.2 22.5 %psum.14 = f32[3,2560]{1,0:T(4,128)S(1)} all-reduce(f32[3,2560]{1,0:T(4,128)S(1)} %pad_maximum_fusion.5), channel_id=1, replica_groups=mesh['seq'=64,'head'=8] {'head'}, use_global_device_ids=true, to_apply=%region_22.23 | all-reduce | flops 7680 | bytes 61440 | tf_op jit(solution)/shard_map/psum | solution.py:245
  1112.7 248.2 %psum.15 = f32[3,2560]{1,0:T(4,128)} all-reduce(f32[3,2560]{1,0:T(4,128)S(1)} %psum.14), channel_id=1, replica_groups=mesh['seq'=64,'head'=8] {'seq'}, use_global_device_ids=true, to_apply=%region_23.24 | all-reduce | flops 7680 | bytes 61440 | tf_op jit(solution)/shard_map/psum | solution.py:245
  1362.5 4.3 fusion.77
  (805 shorter events, 610.6 us)
Async XLA Ops:
  8.1 8.5 collective-permute-start
  16.6 3.5 copy-start.3
  17.0 3.1 copy-start.5
  20.1 6.9 copy-start.17
  20.1 6.9 copy-start.16
  20.1 40.9 %all-to-all-start = ((f32[128,8,320]{0,2,1:T(8,128)}), f32[128,8,320]{0,2,1:T(8,128)S(1)}, u32[]{:S(2)}, u32[]{:S(2)}) async-start(f32[128,8,320]{0,2,1:T(8,128)} %bitcast.265), calls=%async_computation | async-start | bytes 2621440 | tf_op jit(solution)/shard_map/all_to_all | solution.py:235
  26.2 261.4 %all-gather.9.cloned.1.call-start = ((), (), s32[]{:S(2)}) async-start(), calls=%async_computation.3 | async-start | bytes 10649600 | tf_op jit(solution)/shard_map/all_gather | solution.py:15
  26.3 66.4 %copy-start.15 = (s32[1026]{0:T(1024)}, s32[1026]{0:T(1024)S(1)}, u32[]{:S(2)}) copy-start(s32[1026]{0:T(1024)S(1)} %select_reduce_fusion) | copy-start | bytes 12316
  73.9 3.1 copy-start.18
  84.7 2.3 copy-start.14
  88.4 138.1 %all-to-all-start.1 = ((f32[128,8,256]{0,2,1:T(8,128)}), f32[128,8,256]{0,2,1:T(8,128)S(1)}, u32[]{:S(2)}, u32[]{:S(2)}) async-start(f32[128,8,256]{0,2,1:T(8,128)} %bitcast.273), calls=%async_computation.1 | async-start | bytes 2097152 | tf_op jit(solution)/shard_map/all_to_all | solution.py:236
  91.9 591.0 %all-gather.11.cloned.1.call-start = ((), (), s32[]{:S(2)}) async-start(), calls=%async_computation.4 | async-start | bytes 10649600 | tf_op jit(solution)/shard_map/all_gather | solution.py:15
  230.5 1.7 copy-start.10
  231.6 1.4 copy-start.9
  475.3 1.2 slice-start.1
  589.0 2.9 copy-start.2
  590.9 1.0 copy-start
  986.2 1.7 copy-start.8
  989.7 3.1 copy-start.7
  991.6 7.0 copy-start.1
  998.6 14.0 %copy-start.13 = (f32[136,2,1024]{2,1,0:T(2,128)S(1)}, f32[136,2,1024]{2,1,0:T(2,128)}, u32[]{:S(2)}) copy-start(f32[136,2,1024]{2,1,0:T(2,128)} %get-tuple-element.1102) | copy-start | bytes 3342340
  1020.3 1.4 copy-start.12
  1021.7 7.6 slice-start
  1021.7 7.6 copy-start.11
  1044.8 40.9 %copy-start.4 = (f32[128,2560]{0,1:T(8,128)S(1)}, f32[128,2560]{0,1:T(8,128)}, u32[]{:S(2)}) copy-start(f32[128,2560]{0,1:T(8,128)} %copy-done.3) | copy-start | bytes 3932164
  1044.8 40.8 %copy-start.6 = (f32[2,2560]{0,1:T(8,128)S(1)}, f32[2,2560]{0,1:T(8,128)}, u32[]{:S(2)}) copy-start(f32[2,2560]{0,1:T(8,128)} %copy-done.5) | copy-start | bytes 61444
  1088.2 272.7 %collective-permute-start.1 = (f32[2,2560]{1,0:T(2,128)S(1)}, f32[2,2560]{1,0:T(2,128)S(1)}, u32[]{:S(2)}, u32[]{:S(2)}) collective-permute-start(f32[2,2560]{1,0:T(2,128)S(1)} %copy.144), channel_id=1, source_target_pairs={{1,0},{2,1},{3,2},{4,3},{5,4},{6,5},{7,6},{8,7},{9,8},{10,9},{11,1... | collective-permute-start | bytes 61448 | tf_op jit(solution)/shard_map/ppermute | solution.py:32
Sparse Core Ops, SparseCore 0:
  87.2 91.7 all-gather.8
  594.3 88.6 all-gather.10
